TPU v7x, 128 devices: a whole 4x4x4 slice. The times are simulated.
128 devices in a mesh: expert: 16 (over z, x), dp: 8 (over y, core).
Axes of the slice: x: 4, y: 4, z: 4, core: 2. Of those that a mesh axis runs over, the one named last changes fastest.
Arguments:
- tokens: bfloat16 [16, 480, 7168], P('expert', 'dp'), may hold values from -6 to 6
- cotangent: bfloat16 [16, 480, 7168], P('expert', 'dp'), may hold values from -1.5 to 1.5
- counts: int32 [16, 8], replicated, may hold values from 1 to 60, as said below
- w_gate: bfloat16 [16, 7168, 2048], P('expert', None, 'dp'), may hold values from -0.0625 to 0.0625
- w_up: bfloat16 [16, 7168, 2048], P('expert', None, 'dp'), may hold values from -0.0625 to 0.0625
- w_down: bfloat16 [16, 2048, 7168], P('expert', 'dp'), may hold values from -0.125 to 0.125
Outputs:
- outputs: bfloat16 [16, 480, 7168], P('expert', 'dp')
- input_grads: bfloat16 [16, 480, 7168], P('expert', 'dp')
- gate_grad: bfloat16 [16, 7168, 2048], P('expert', None, 'dp')
- up_grad: bfloat16 [16, 7168, 2048], P('expert', None, 'dp')
- down_grad: bfloat16 [16, 2048, 7168], P('expert', 'dp')
Inputs may be any that keep to these rules, and one draw needn't show every extreme that they name: For each expert e below 8, exactly one of experts e and e + 8 is hot: all its counts exceed 40 - 20 and one equals 60; every count of the other is at most 20 and one equals 20.
All inputs are finite; a program needn't handle non-finite values.
Results may differ from a plain program's by a relative error of at most 0.012.
Values may be sent and summed in bfloat16 or wider, within the bound.
No kernel may reach another device: no remote copies, remote signals or barrier semaphores. Data moves between devices by JAX's collectives and lax.ppermute only.
A program may use at most 192 MiB of HBM per device.

v0:
```python
import jax
import jax.numpy as jnp
from jax import lax
from jax.sharding import PartitionSpec as P


def silu_slope(value):
    sigma = jax.nn.sigmoid(value)
    return sigma * (1.0 + value * (1.0 - sigma))


def contract_last(left, right):
    return lax.dot_general(
        left, right, (((1,), (1,)), ((), ())), preferred_element_type=jnp.float32
    )


def contract_first(left, right):
    return lax.dot_general(
        left, right, (((0,), (0,)), ((), ())), preferred_element_type=jnp.float32
    )


def expert_work(rows, cot_rows, gate_w, up_w, down_w):
    gate = jnp.dot(rows, gate_w, preferred_element_type=jnp.float32)
    up = jnp.dot(rows, up_w, preferred_element_type=jnp.float32)
    active = jax.nn.silu(gate)
    hidden = (active * up).astype(jnp.bfloat16)
    out_part = jnp.dot(hidden, down_w, preferred_element_type=jnp.float32).astype(jnp.bfloat16)
    out_part, hidden, gate, up = lax.optimization_barrier((out_part, hidden, gate, up))
    active = jax.nn.silu(gate)
    hidden_grad = contract_last(cot_rows, down_w)
    gate_act = (hidden_grad * up * silu_slope(gate)).astype(jnp.bfloat16)
    up_act = (hidden_grad * active).astype(jnp.bfloat16)
    in_part = contract_last(gate_act, gate_w) + contract_last(up_act, up_w)
    gate_term = contract_first(rows, gate_act)
    up_term = contract_first(rows, up_act)
    down_term = contract_first(hidden, cot_rows)
    return (out_part, in_part, gate_term, up_term, down_term)


def shards(tokens, cotangent, counts, w_gate, w_up, w_down):
    rows_in = tokens[0]
    cot_in = cotangent[0]
    gate_w = w_gate[0]
    up_w = w_up[0]
    down_w = w_down[0]
    expert_pos = lax.axis_index("expert")
    batch_pos = lax.axis_index("dp")
    expert_ids = jnp.arange(counts.shape[0], dtype=jnp.int32)
    batch_ids = jnp.arange(counts.shape[1], dtype=jnp.int32)
    own_counts = jnp.sum(jnp.where(expert_ids[:, None] == expert_pos, counts, 0), axis=0)
    own_total = jnp.sum(jnp.where(batch_ids == batch_pos, own_counts, 0))
    slots = rows_in.shape[0]
    valid = (jnp.arange(slots, dtype=jnp.int32) < own_total)[:, None]
    masked = jnp.where(valid, rows_in, jnp.zeros_like(rows_in))
    masked_cot = jnp.where(valid, cot_in, jnp.zeros_like(cot_in))
    all_rows = lax.all_gather(masked, "dp", axis=0, tiled=True)
    all_cot = lax.all_gather(masked_cot, "dp", axis=0, tiled=True)
    out_part, in_part, gate_term, up_term, down_term = expert_work(
        all_rows, all_cot, gate_w, up_w, down_w
    )
    groups = lax.axis_size("dp")
    outputs = lax.psum_scatter(
        out_part.reshape(groups, slots, -1), "dp", scatter_dimension=0, tiled=False
    )
    input_grads = lax.psum_scatter(
        in_part.astype(jnp.bfloat16).reshape(groups, slots, -1),
        "dp",
        scatter_dimension=0,
        tiled=False,
    )
    gate_grad = gate_term.astype(jnp.bfloat16)
    up_grad = up_term.astype(jnp.bfloat16)
    down_grad = down_term.astype(jnp.bfloat16)
    return (outputs[None], input_grads[None], gate_grad[None], up_grad[None], down_grad[None])


def solution(mesh):
    placed = (
        P("expert", "dp", None),
        P("expert", "dp", None),
        P(),
        P("expert", None, "dp"),
        P("expert", None, "dp"),
        P("expert", "dp", None),
    )
    return jax.shard_map(
        shards,
        mesh=mesh,
        in_specs=placed,
        out_specs=(
            P("expert", "dp", None),
            P("expert", "dp", None),
            P("expert", None, "dp"),
            P("expert", None, "dp"),
            P("expert", "dp", None),
        ),
        check_vma=False,
    )
```

profile of v0, /device:TPU:1, one launch (start us, length us, event | category | flops | bytes accessed | tf_op | source)
XLA Modules:
  0.0 215.1 jit_solution(16203403560469040614)
XLA Ops:
  7.2 0.0 all-gather.5.cloned.1.call-start
  7.2 0.8 select_reduce_fusion
  8.0 0.6 fusion.15
  8.7 0.6 iota_compare_fusion.1
  9.3 2.9 %fusion.13 = (bf16[1,60,7168]{2,1,0:T(8,128)(2,1)}, bf16[1,60,7168]{2,1,0:T(8,128)(2,1)}) fusion(bf16[1,60,7168]{2,1,0:T(8,128)(2,1)} %param.7, pred[60]{0:T(512)(128)(4,1)S(1)} %iota_compare_fusion.1, bf16[1,60,7168]{2,1,0:T(8,128)(2,1)} %param.6), kind=kLoop, calls=%fused_computation.19 | loop fusion | flops 860160 | bytes 3440700
  12.2 0.0 all-gather.5.cloned.1.call-update
  12.2 0.0 all-gather.7.cloned.1.call-start
  12.3 0.7 all-gather.7.cloned.1.call-update
  13.0 0.0 reduce-scatter.3.cloned.1.call-start
  13.0 48.2 %all-gather.5.cloned.1.call-done = bf16[8,60,7168]{2,1,0:T(8,128)(2,1)} async-done(((bf16[1,60,7168]{2,1,0:T(8,128)(2,1)}), bf16[8,60,7168]{2,1,0:T(8,128)(2,1)}) %all-gather.5.cloned.1.call-update) | async-done | bytes 6881296 | tf_op jit(solution)/shard_map/all_gather | solution.py:58
  61.3 6.9 %reshape.28 = bf16[480,7168]{1,0:T(8,128)(2,1)} reshape(bf16[8,60,7168]{2,1,0:T(8,128)(2,1)} %all-gather.5.cloned.1.call-done) | data formatting | bytes 13762560
  68.2 0.0 copy-start
  68.2 0.0 copy-start.1
  68.2 6.2 %fusion.11 = f32[480,256]{1,0:T(8,128)S(1)} fusion(bf16[480,7168]{1,0:T(8,128)(2,1)} %reshape.28, bf16[1,7168,256]{2,1,0:T(8,128)(2,1)} %param.9), kind=kOutput, calls=%fused_computation.16 | convolution fusion | flops 1761607680 | bytes 11042816 | tf_op jit(solution)/shard_map/dot_general | solution.py:25
  74.3 0.4 copy-done
  74.8 1.6 copy-done.1
  76.4 0.0 copy-start.3
  76.4 1.9 multiply_convert_fusion.2
  78.4 0.1 copy-done.3
  78.4 4.8 %convolution_convert_fusion = bf16[480,7168]{1,0:T(8,128)(2,1)} fusion(bf16[480,256]{1,0:T(8,128)(2,1)S(1)} %get-tuple-element.12, bf16[1,256,7168]{2,1,0:T(8,128)(2,1)S(1)} %copy-done.3), kind=kOutput, calls=%fused_computation.1 | convolution fusion | flops 1765048320 | bytes 10797056 | tf_op jit(solution)/shard_map/dot_general | solution.py:29
  83.2 6.9 %reshape.25 = bf16[8,60,7168]{2,1,0:T(8,128)(2,1)} reshape(bf16[480,7168]{1,0:T(8,128)(2,1)} %convolution_convert_fusion) | data formatting | bytes 13762560 | tf_op jit(solution)/shard_map/reshape | solution.py:65
  90.1 0.0 reduce-scatter.3.cloned.1.call-update
  90.2 0.2 reduce-scatter.5.cloned.1.call-start
  90.4 18.5 %all-gather.7.cloned.1.call-done = bf16[8,60,7168]{2,1,0:T(8,128)(2,1)} async-done(((bf16[1,60,7168]{2,1,0:T(8,128)(2,1)}), bf16[8,60,7168]{2,1,0:T(8,128)(2,1)}) %all-gather.7.cloned.1.call-update) | async-done | bytes 6881296 | tf_op jit(solution)/shard_map/all_gather | solution.py:59
  108.9 6.8 %reshape.30 = bf16[480,7168]{1,0:T(8,128)(2,1)} reshape(bf16[8,60,7168]{2,1,0:T(8,128)(2,1)} %all-gather.7.cloned.1.call-done) | data formatting | bytes 13762560
  115.7 0.0 copy-start.4
  115.7 6.2 %multiply_convert_fusion = (bf16[480,256]{1,0:T(8,128)(2,1)S(1)}, bf16[480,256]{1,0:T(8,128)(2,1)S(1)}) fusion(f32[480,256]{1,0:T(8,128)S(1)} %fusion.11, f32[480,256]{1,0:T(8,128)S(1)} %get-tuple-element.10, bf16[480,7168]{1,0:T(8,128)(2,1)} %reshape.30, bf16[1,256,7168]{2,1,0:T(8,128)(2,1)} %param.11), kind=kOutput, calls=%fused_computation.22 | convolution fusion | flops 1763205120 | bytes 12025856 | tf_op jit(solution)/shard_map/dot_general | solution.py:13
  121.9 0.0 copy-done.4
  121.9 0.0 copy-start.2
  121.9 6.9 %fusion.9 = f32[480,7168]{1,0:T(8,128)} fusion(bf16[480,256]{1,0:T(8,128)(2,1)S(1)} %get-tuple-element.14, bf16[1,7168,256]{2,1,0:T(8,128)(2,1)S(1)} %copy-done.4), kind=kOutput, calls=%fused_computation.14 | convolution fusion | flops 1761607680 | bytes 17678336 | tf_op jit(solution)/shard_map/dot_general | solution.py:13
  128.8 0.0 copy-done.2
  128.8 10.0 %add_convert_fusion = bf16[480,7168]{1,0:T(8,128)(2,1)} fusion(f32[480,7168]{1,0:T(8,128)} %fusion.9, bf16[480,256]{1,0:T(8,128)(2,1)S(1)} %get-tuple-element.13, bf16[1,7168,256]{2,1,0:T(8,128)(2,1)S(1)} %copy-done.2), kind=kOutput, calls=%fused_computation | convolution fusion | flops 1768488960 | bytes 24559616 | tf_op jit(solution)/shard_map/dot_general | solution.py:13
  138.9 7.0 %reshape.26 = bf16[8,60,7168]{2,1,0:T(8,128)(2,1)} reshape(bf16[480,7168]{1,0:T(8,128)(2,1)} %add_convert_fusion) | data formatting | bytes 13762560 | tf_op jit(solution)/shard_map/reshape | solution.py:68
  145.8 0.0 slice-start
  145.8 0.0 reduce-scatter.5.cloned.1.call-update
  145.9 0.0 slice-start.1
  145.9 7.2 %fusion.2 = bf16[1,256,7168]{2,1,0:T(8,128)(2,1)} fusion(bf16[480,256]{1,0:T(8,128)(2,1)S(1)} %get-tuple-element.12, bf16[480,7168]{1,0:T(8,128)(2,1)} %reshape.30), kind=kOutput, calls=%fused_computation.7 | convolution fusion | flops 1763442688 | bytes 10797056 | tf_op jit(solution)/shard_map/dot_general | solution.py:19
  153.1 0.0 slice-done
  153.1 0.0 slice-done.1
  153.1 4.0 %fusion.1 = bf16[1,7168,256]{2,1,0:T(8,128)(2,1)} fusion(bf16[480,7168]{1,0:T(8,128)(2,1)S(1)} %bitcast.50, bf16[480,256]{1,0:T(8,128)(2,1)S(1)} %get-tuple-element.13), kind=kOutput, calls=%fused_computation.6 | convolution fusion | flops 1763442688 | bytes 10797056 | tf_op jit(solution)/shard_map/dot_general | solution.py:19
  157.1 4.0 %fusion = bf16[1,7168,256]{2,1,0:T(8,128)(2,1)} fusion(bf16[480,7168]{1,0:T(8,128)(2,1)S(1)} %bitcast.50, bf16[480,256]{1,0:T(8,128)(2,1)S(1)} %get-tuple-element.14), kind=kOutput, calls=%fused_computation.5 | convolution fusion | flops 1763442688 | bytes 10797056 | tf_op jit(solution)/shard_map/dot_general | solution.py:19
  161.1 0.0 reduce-scatter.3.cloned.1.call-done
  161.1 47.4 %reduce-scatter.5.cloned.1.call-done = bf16[1,60,7168]{2,1,0:T(8,128)(2,1)} async-done(((bf16[8,60,7168]{2,1,0:T(8,128)(2,1)}), bf16[1,60,7168]{2,1,0:T(8,128)(2,1)}) %reduce-scatter.5.cloned.1.call-update) | async-done | bytes 860176 | tf_op jit(solution)/shard_map/reduce_scatter | solution.py:67
  (2 shorter events, 0.0 us)
Async XLA Ops:
  7.2 54.1 %all-gather.5.cloned.1.call-start = ((), (), s32[]{:S(2)}) async-start(), calls=%async_computation.4 | async-start | bytes 8257536 | tf_op jit(solution)/shard_map/all_gather | solution.py:58
  12.2 96.7 %all-gather.7.cloned.1.call-start = ((), (), s32[]{:S(2)}) async-start(), calls=%async_computation.5 | async-start | bytes 8257536 | tf_op jit(solution)/shard_map/all_gather | solution.py:59
  13.0 148.2 %reduce-scatter.3.cloned.1.call-start = ((), (), s32[]{:S(2)}) async-start(), calls=%async_computation.2 | async-start | bytes 8257536 | tf_op jit(solution)/shard_map/reduce_scatter | solution.py:64
  68.2 6.6 %copy-start = (bf16[480,7168]{1,0:T(8,128)(2,1)S(1)}, bf16[480,7168]{1,0:T(8,128)(2,1)}, u32[]{:S(2)}) copy-start(bf16[480,7168]{1,0:T(8,128)(2,1)} %reshape.28) | copy-start | bytes 20643844
  68.2 8.2 %copy-start.1 = (bf16[1,7168,256]{2,1,0:T(8,128)(2,1)S(1)}, bf16[1,7168,256]{2,1,0:T(8,128)(2,1)}, u32[]{:S(2)}) copy-start(bf16[1,7168,256]{2,1,0:T(8,128)(2,1)} %param.10) | copy-start | bytes 11010052
  76.4 2.0 copy-start.3
  90.2 118.4 %reduce-scatter.5.cloned.1.call-start = ((), (), s32[]{:S(2)}) async-start(), calls=%async_computation.3 | async-start | bytes 8257536 | tf_op jit(solution)/shard_map/reduce_scatter | solution.py:67
  115.7 6.2 %copy-start.4 = (bf16[1,7168,256]{2,1,0:T(8,128)(2,1)S(1)}, bf16[1,7168,256]{2,1,0:T(8,128)(2,1)}, u32[]{:S(2)}) copy-start(bf16[1,7168,256]{2,1,0:T(8,128)(2,1)} %param.9) | copy-start | bytes 11010052
  121.9 7.0 %copy-start.2 = (bf16[1,7168,256]{2,1,0:T(8,128)(2,1)S(1)}, bf16[1,7168,256]{2,1,0:T(8,128)(2,1)}, u32[]{:S(2)}) copy-start(bf16[1,7168,256]{2,1,0:T(8,128)(2,1)} %param.10) | copy-start | bytes 11010052
  145.8 7.2 %slice-start = ((s8[6881280]{0:T(1024)(128)(4,1)}), s8[2686976]{0:T(1024)(128)(4,1)S(1)}, s32[]{:S(2)}) async-start(s8[6881280]{0:T(1024)(128)(4,1)} %bitcast.49), calls=%async_computation.6 | async-start | bytes 5373952
  145.9 7.2 %slice-start.1 = ((s8[6881280]{0:T(1024)(128)(4,1)}), s8[4194304]{0:T(1024)(128)(4,1)S(1)}, s32[]{:S(2)}) async-start(s8[6881280]{0:T(1024)(128)(4,1)} %bitcast.49), calls=%async_computation.7 | async-start | bytes 8388608
Sparse Core Ops, SparseCore 0:
  12.3 48.8 all-gather.4
  63.5 45.3 all-gather.6
  111.9 46.6 reduce-scatter.2
  161.4 47.0 reduce-scatter.4
where the time goes:
time: 215 us
  waiting for transfers between devices  115 us (53%)
  matrix products  51.3 us (24%)
  local copies, waits for them, and re-layouts  29.7 us (14%)
  between operations  13.8 us (6%)
  other arithmetic  4.97 us (2%)
    all_gather x1, waiting for transfers between devices, shards(): all_rows = lax.all_gather(masked, 'dp', axis=0, tiled=True)  48.2 us
    reduce_scatter x1, waiting for transfers between devices, shards(): lax.psum_scatter(in_part.astype(jnp.bfloat16).reshape(groups, slots, -1),...  47.4 us
    dot_general x3, matrix products, contract_last(): lax.dot_general(left, right, (((1,), (1,)), ((), ())), preferred_element_...  23.2 us
    all_gather x1, waiting for transfers between devices, shards(): all_cot = lax.all_gather(masked_cot, 'dp', axis=0, tiled=True)  18.5 us
    unnamed x16, local copies, waits for them, and re-layouts  15.9 us
    dot_general x3, matrix products, contract_first(): lax.dot_general(left, right, (((0,), (0,)), ((), ())), preferred_element_...  15.2 us
    reshape x1, local copies, waits for them, and re-layouts, shards(): in_part.astype(jnp.bfloat16).reshape(groups, slots, -1)  6.95 us
    reshape x1, local copies, waits for them, and re-layouts, shards(): out_part.reshape(groups, slots, -1)  6.9 us
  transfers between devices with their start and end apart: 4, of which 3 were waited for; matrix products, arithmetic and copies ran while one was open for 37% of the time, Pallas kernels for 0%

commit v1 on v0

--- a/solution.py
+++ b/solution.py
@@ -56,7 +56,28 @@
     masked = jnp.where(valid, rows_in, jnp.zeros_like(rows_in))
     masked_cot = jnp.where(valid, cot_in, jnp.zeros_like(cot_in))
     all_rows = lax.all_gather(masked, "dp", axis=0, tiled=True)
-    all_cot = lax.all_gather(masked_cot, "dp", axis=0, tiled=True)
+    passed, d_next, earlier = (lax.axis_size("dp"), lax.axis_index("dp"), masked_cot.shape[0])
+    runs = tuple((p * passed if src_i == 0 else p for src_i, p in enumerate(masked_cot.shape)))
+    all_cot = lax.dynamic_update_slice_in_dim(
+        jnp.zeros(runs, masked_cot.dtype), masked_cot, d_next * earlier, axis=0
+    )
+    carry_out = z_new = masked_cot
+    to_i = 1
+    while to_i < passed // 2 + 1:
+        carry_out = lax.ppermute(
+            carry_out, "dp", tuple(((src_i, (src_i + 1) % passed) for src_i in range(passed)))
+        )
+        all_cot = lax.dynamic_update_slice_in_dim(
+            all_cot, carry_out, (d_next - to_i) % passed * earlier, axis=0
+        )
+        if 2 * to_i < passed:
+            z_new = lax.ppermute(
+                z_new, "dp", tuple(((src_i, (src_i - 1) % passed) for src_i in range(passed)))
+            )
+            all_cot = lax.dynamic_update_slice_in_dim(
+                all_cot, z_new, (d_next + to_i) % passed * earlier, axis=0
+            )
+        to_i += 1
     out_part, in_part, gate_term, up_term, down_term = expert_work(
         all_rows, all_cot, gate_w, up_w, down_w
     )

time: 215 us -> 280 us (1.30)
  local copies, waits for them, and re-layouts: 29.7 us -> 62 us
  waiting for transfers between devices: 115 us -> 132 us
  starting transfers between devices: 0.34 us -> 14.4 us
    ppermute x0 -> x7, waiting for transfers between devices: none -> 47.4 us  [the longest x4 45.8 us: shards(): lax.ppermute(carry_out, 'dp', tuple(((src_i, (src_i + 1) % passed) for sr...]
    dynamic_update_slice x0 -> x8, local copies, waits for them, and re-layouts: none -> 36.9 us  [the longest x4 18.1 us: shards(): lax.dynamic_update_slice_in_dim(all_cot, carry_out, (d_next - to_i) % pas...]
    all_gather x1 -> x0, waiting for transfers between devices: 18.5 us -> none  [shards(): all_cot = lax.all_gather(masked_cot, 'dp', axis=0, tiled=True)]
    ppermute x0 -> x7, starting transfers between devices: none -> 14.1 us  [the longest x4 8.05 us: shards(): lax.ppermute(carry_out, 'dp', tuple(((src_i, (src_i + 1) % passed) for sr...]
    reduce_scatter x1, waiting for transfers between devices: 47.4 us -> 35.6 us  [shards(): lax.psum_scatter(in_part.astype(jnp.bfloat16).reshape(groups, slots, -1),...]
    unnamed x16 -> x21, local copies, waits for them, and re-layouts: 15.9 us -> 7.86 us
    broadcast_in_dim x0 -> x1, local copies, waits for them, and re-layouts: none -> 3.59 us  [shards(): jnp.zeros(runs, masked_cot.dtype)]
    unnamed x2 -> x1, other arithmetic: 2.87 us -> 0.01 us
  transfers between devices with their start and end apart: 4 -> 10, of which waited for: 3 -> 7; matrix products, arithmetic and copies ran while one was open for 37% -> 31% of each run, Pallas kernels for 0% -> 0%
where the time goes in v1:
time: 280 us; the launch traced here: 279 us
  waiting for transfers between devices  132 us (47%)
  local copies, waits for them, and re-layouts  62 us (22%)
  matrix products  51.6 us (18%)
  starting transfers between devices  14.4 us (5%)
  between operations  13.8 us (5%)
  other arithmetic  4.67 us (2%)
    all_gather x1, waiting for transfers between devices, shards(): all_rows = lax.all_gather(masked, 'dp', axis=0, tiled=True)  49 us
    ppermute x4, waiting for transfers between devices, shards(): lax.ppermute(carry_out, 'dp', tuple(((src_i, (src_i + 1) % passed) for sr...  45.8 us
    reduce_scatter x1, waiting for transfers between devices, shards(): lax.psum_scatter(in_part.astype(jnp.bfloat16).reshape(groups, slots, -1),...  35.6 us
    dot_general x3, matrix products, contract_last(): lax.dot_general(left, right, (((1,), (1,)), ((), ())), preferred_element_...  22.9 us
    dynamic_update_slice x4, local copies, waits for them, and re-layouts, shards(): lax.dynamic_update_slice_in_dim(all_cot, carry_out, (d_next - to_i) % pas...  18.1 us
    dot_general x3, matrix products, contract_first(): lax.dot_general(left, right, (((0,), (0,)), ((), ())), preferred_element_...  15.1 us
    dynamic_update_slice x3, local copies, waits for them, and re-layouts, shards(): lax.dynamic_update_slice_in_dim(all_cot, z_new, (d_next + to_i) % passed...  14.3 us
    ppermute x4, starting transfers between devices, shards(): lax.ppermute(carry_out, 'dp', tuple(((src_i, (src_i + 1) % passed) for sr...  8.05 us
  transfers between devices with their start and end apart: 10, of which 7 were waited for; matrix products, arithmetic and copies ran while one was open for 31% of the time, Pallas kernels for 0%

profile of v1, /device:TPU:1, one launch (start us, length us, event | category | flops | bytes accessed | tf_op | source)
XLA Modules:
  0.0 278.5 jit_solution(18351495931752930758)
XLA Ops:
  7.2 0.0 all-gather.3.cloned.1.call-start
  7.2 0.8 select_reduce_fusion
  8.0 0.6 fusion.14
  8.7 0.6 iota_compare_fusion.1
  9.3 2.6 bitcast_select_fusion
  11.9 0.0 all-gather.3.cloned.1.call-update
  11.9 0.0 reduce-scatter.3.cloned.1.call-start
  12.0 49.0 %all-gather.3.cloned.1.call-done = bf16[8,60,7168]{2,1,0:T(8,128)(2,1)} async-done(((bf16[1,60,7168]{2,1,0:T(8,128)(2,1)}), bf16[8,60,7168]{2,1,0:T(8,128)(2,1)}) %all-gather.3.cloned.1.call-update) | async-done | bytes 6881296 | tf_op jit(solution)/shard_map/all_gather | solution.py:58
  60.9 6.9 %reshape.28 = bf16[480,7168]{1,0:T(8,128)(2,1)} reshape(bf16[8,60,7168]{2,1,0:T(8,128)(2,1)} %all-gather.3.cloned.1.call-done) | data formatting | bytes 13762560
  67.9 0.0 copy-start
  67.9 0.0 copy-start.1
  67.9 6.1 %fusion.11 = f32[480,256]{1,0:T(8,128)S(1)} fusion(bf16[480,7168]{1,0:T(8,128)(2,1)} %reshape.28, bf16[1,7168,256]{2,1,0:T(8,128)(2,1)} %param.9), kind=kOutput, calls=%fused_computation.16 | convolution fusion | flops 1761607680 | bytes 11042816 | tf_op jit(solution)/shard_map/dot_general | solution.py:25
  74.0 0.0 copy-done
  74.0 0.9 copy-done.1
  74.9 0.0 copy-start.3
  74.9 2.7 multiply_convert_fusion.2
  77.6 0.0 copy-done.3
  77.6 4.8 %convolution_convert_fusion = bf16[480,7168]{1,0:T(8,128)(2,1)} fusion(bf16[480,256]{1,0:T(8,128)(2,1)S(1)} %get-tuple-element.12, bf16[1,256,7168]{2,1,0:T(8,128)(2,1)S(1)} %copy-done.3), kind=kOutput, calls=%fused_computation.1 | convolution fusion | flops 1765048320 | bytes 10797056 | tf_op jit(solution)/shard_map/dot_general | solution.py:29
  82.4 6.8 %reshape.25 = bf16[8,60,7168]{2,1,0:T(8,128)(2,1)} reshape(bf16[480,7168]{1,0:T(8,128)(2,1)} %convolution_convert_fusion) | data formatting | bytes 13762560 | tf_op jit(solution)/shard_map/reshape | solution.py:86
  89.2 0.0 reduce-scatter.3.cloned.1.call-update
  89.2 0.2 reduce-scatter.5.cloned.1.call-start
  89.5 0.5 collective-permute-start
  90.0 0.0 collective-permute-start.1
  90.0 12.9 %collective-permute-done = bf16[60,7168]{1,0:T(8,128)(2,1)S(1)} collective-permute-done((bf16[60,7168]{1,0:T(8,128)(2,1)S(1)}, bf16[60,7168]{1,0:T(8,128)(2,1)S(1)}, u32[]{:S(2)}, u32[]{:S(2)}) %collective-permute-start) | collective-permute-done | bytes 860192 | tf_op jit(solution)/shard_map/ppermute | solution.py:67
  102.9 2.5 collective-permute-start.2
  105.4 0.6 collective-permute-done.1
  106.0 0.0 copy-start.5
  106.0 2.6 collective-permute-start.3
  108.6 17.0 %collective-permute-done.2 = bf16[60,7168]{1,0:T(8,128)(2,1)S(1)} collective-permute-done((bf16[60,7168]{1,0:T(8,128)(2,1)S(1)}, bf16[60,7168]{1,0:T(8,128)(2,1)S(1)}, u32[]{:S(2)}, u32[]{:S(2)}) %collective-permute-start.2) | collective-permute-done | bytes 860192 | tf_op jit(solution)/shard_map/ppermute | solution.py:67
  125.6 0.0 copy-done.5
  125.6 0.0 copy-start.6
  125.6 2.5 collective-permute-start.4
  128.1 1.0 collective-permute-done.3
  129.1 0.0 copy-done.6
  129.1 3.4 %collective-permute-start.5 = (bf16[60,7168]{1,0:T(8,128)(2,1)}, bf16[60,7168]{1,0:T(8,128)(2,1)}, u32[]{:S(2)}, u32[]{:S(2)}) collective-permute-start(bf16[60,7168]{1,0:T(8,128)(2,1)} %collective-permute-done.3), channel_id=1, source_target_pairs={{0,7},{1,0},{2,1},{3,2},{4,3},{5,4},{6,5},{7,6},{8,15},{9,8},{10,9... | collective-permute-start | bytes 2580488 | tf_op jit(solution)/shard_map/ppermute | solution.py:74
  132.5 15.8 %collective-permute-done.4 = bf16[60,7168]{1,0:T(8,128)(2,1)} collective-permute-done((bf16[60,7168]{1,0:T(8,128)(2,1)S(1)}, bf16[60,7168]{1,0:T(8,128)(2,1)}, u32[]{:S(2)}, u32[]{:S(2)}) %collective-permute-start.4) | collective-permute-done | bytes 860192 | tf_op jit(solution)/shard_map/ppermute | solution.py:67
  148.4 2.6 collective-permute-start.6
  150.9 3.6 %broadcast_in_dim.45 = bf16[480,7168]{1,0:T(8,128)(2,1)} broadcast(bf16[]{:T(256)} %constant.61.clone.1), dimensions={} | broadcast | bytes 6881282 | tf_op jit(solution)/shard_map/broadcast_in_dim | solution.py:62
  154.5 4.5 %dynamic_update_slice.24 = bf16[480,7168]{1,0:T(8,128)(2,1)} dynamic-update-slice(bf16[480,7168]{1,0:T(8,128)(2,1)} %broadcast_in_dim.45, bf16[60,7168]{1,0:T(8,128)(2,1)S(1)} %get-tuple-element.15, s32[]{:T(128)S(6)} %select_n.74, s32[]{:T(128)} %constant.60.clone.1) | dynamic-update-slice | bytes 1720324 | tf_op jit(solution)/shard_map/dynamic_update_slice | solution.py:61
  159.0 4.5 %dynamic_update_slice.25 = bf16[480,7168]{1,0:T(8,128)(2,1)} dynamic-update-slice(bf16[480,7168]{1,0:T(8,128)(2,1)} %dynamic_update_slice.24, bf16[60,7168]{1,0:T(8,128)(2,1)S(1)} %collective-permute-done, s32[]{:T(128)S(6)} %select_n.76, s32[]{:T(128)} %constant.60.clone.1) | dynamic-update-slice | bytes 1720324 | tf_op jit(solution)/shard_map/dynamic_update_slice | solution.py:70
  163.5 4.8 %dynamic_update_slice.26 = bf16[480,7168]{1,0:T(8,128)(2,1)} dynamic-update-slice(bf16[480,7168]{1,0:T(8,128)(2,1)} %dynamic_update_slice.25, bf16[60,7168]{1,0:T(8,128)(2,1)} %copy-done.5, s32[]{:T(128)S(6)} %select_n.78, s32[]{:T(128)} %constant.60.clone.1) | dynamic-update-slice | bytes 1720324 | tf_op jit(solution)/shard_map/dynamic_update_slice | solution.py:77
  168.3 4.0 %dynamic_update_slice.27 = bf16[480,7168]{1,0:T(8,128)(2,1)} dynamic-update-slice(bf16[480,7168]{1,0:T(8,128)(2,1)} %dynamic_update_slice.26, bf16[60,7168]{1,0:T(8,128)(2,1)} %copy-done.6, s32[]{:T(128)S(6)} %select_n.80, s32[]{:T(128)} %constant.60.clone.1) | dynamic-update-slice | bytes 1720324 | tf_op jit(solution)/shard_map/dynamic_update_slice | solution.py:70
  172.3 4.8 %dynamic_update_slice.28 = bf16[480,7168]{1,0:T(8,128)(2,1)} dynamic-update-slice(bf16[480,7168]{1,0:T(8,128)(2,1)} %dynamic_update_slice.27, bf16[60,7168]{1,0:T(8,128)(2,1)} %collective-permute-done.3, s32[]{:T(128)S(6)} %select_n.82, s32[]{:T(128)} %constant.60.clone.1) | dynamic-update-slice | bytes 1720324 | tf_op jit(solution)/shard_map/dynamic_update_slice | solution.py:77
  177.1 4.8 %dynamic_update_slice.29 = bf16[480,7168]{1,0:T(8,128)(2,1)} dynamic-update-slice(bf16[480,7168]{1,0:T(8,128)(2,1)} %dynamic_update_slice.28, bf16[60,7168]{1,0:T(8,128)(2,1)} %collective-permute-done.4, s32[]{:T(128)S(6)} %select_n.84, s32[]{:T(128)} %constant.60.clone.1) | dynamic-update-slice | bytes 1720324 | tf_op jit(solution)/shard_map/dynamic_update_slice | solution.py:70
  181.9 0.0 collective-permute-done.5
  181.9 4.8 %dynamic_update_slice.30 = bf16[480,7168]{1,0:T(8,128)(2,1)} dynamic-update-slice(bf16[480,7168]{1,0:T(8,128)(2,1)} %dynamic_update_slice.29, bf16[60,7168]{1,0:T(8,128)(2,1)} %collective-permute-done.5, s32[]{:T(128)S(6)} %select_n.86, s32[]{:T(128)} %constant.60.clone.1) | dynamic-update-slice | bytes 1720324 | tf_op jit(solution)/shard_map/dynamic_update_slice | solution.py:77
  186.7 0.0 collective-permute-done.6
  186.7 4.8 %dynamic_update_slice.31 = bf16[480,7168]{1,0:T(8,128)(2,1)} dynamic-update-slice(bf16[480,7168]{1,0:T(8,128)(2,1)} %dynamic_update_slice.30, bf16[60,7168]{1,0:T(8,128)(2,1)} %collective-permute-done.6, s32[]{:T(128)S(6)} %select_n.88, s32[]{:T(128)} %constant.60.clone.1) | dynamic-update-slice | bytes 1720324 | tf_op jit(solution)/shard_map/dynamic_update_slice | solution.py:70
  191.4 0.0 copy-done.7
  191.4 6.2 %multiply_convert_fusion = (bf16[480,256]{1,0:T(8,128)(2,1)S(1)}, bf16[480,256]{1,0:T(8,128)(2,1)S(1)}) fusion(f32[480,256]{1,0:T(8,128)S(1)} %fusion.11, f32[480,256]{1,0:T(8,128)S(1)} %copy-done.7, bf16[480,7168]{1,0:T(8,128)(2,1)} %dynamic_update_slice.31, bf16[1,256,7168]{2,1,0:T(8,128)(2,1)} %param.11), kind=kOutput, calls=%fused_computation.21 | convolution fusion | flops 1763205120 | bytes 12025856 | tf_op jit(solution)/shard_map/dot_general | solution.py:13
  197.6 0.0 copy-done.4
  197.6 0.0 copy-start.2
  197.6 6.9 %fusion.9 = f32[480,7168]{1,0:T(8,128)} fusion(bf16[480,256]{1,0:T(8,128)(2,1)S(1)} %get-tuple-element.14, bf16[1,7168,256]{2,1,0:T(8,128)(2,1)S(1)} %copy-done.4), kind=kOutput, calls=%fused_computation.14 | convolution fusion | flops 1761607680 | bytes 17678336 | tf_op jit(solution)/shard_map/dot_general | solution.py:13
  204.6 0.0 copy-done.2
  204.6 9.8 %add_convert_fusion = bf16[480,7168]{1,0:T(8,128)(2,1)} fusion(f32[480,7168]{1,0:T(8,128)} %fusion.9, bf16[480,256]{1,0:T(8,128)(2,1)S(1)} %get-tuple-element.13, bf16[1,7168,256]{2,1,0:T(8,128)(2,1)S(1)} %copy-done.2), kind=kOutput, calls=%fused_computation | convolution fusion | flops 1768488960 | bytes 24559616 | tf_op jit(solution)/shard_map/dot_general | solution.py:13
  214.4 6.9 %reshape.26 = bf16[8,60,7168]{2,1,0:T(8,128)(2,1)} reshape(bf16[480,7168]{1,0:T(8,128)(2,1)} %add_convert_fusion) | data formatting | bytes 13762560 | tf_op jit(solution)/shard_map/reshape | solution.py:89
  221.2 0.0 reduce-scatter.5.cloned.1.call-update
  221.2 0.0 slice-start.1
  221.3 7.0 %fusion.2 = bf16[1,256,7168]{2,1,0:T(8,128)(2,1)} fusion(bf16[480,256]{1,0:T(8,128)(2,1)S(1)} %get-tuple-element.12, bf16[480,7168]{1,0:T(8,128)(2,1)} %dynamic_update_slice.31), kind=kOutput, calls=%fused_computation.7 | convolution fusion | flops 1763442688 | bytes 10797056 | tf_op jit(solution)/shard_map/dot_general | solution.py:19
  228.3 0.0 slice-done
  228.3 0.0 slice-done.1
  228.3 4.0 %fusion.1 = bf16[1,7168,256]{2,1,0:T(8,128)(2,1)} fusion(bf16[480,7168]{1,0:T(8,128)(2,1)S(1)} %bitcast.46, bf16[480,256]{1,0:T(8,128)(2,1)S(1)} %get-tuple-element.13), kind=kOutput, calls=%fused_computation.6 | convolution fusion | flops 1763442688 | bytes 10797056 | tf_op jit(solution)/shard_map/dot_general | solution.py:19
  232.3 4.0 %fusion = bf16[1,7168,256]{2,1,0:T(8,128)(2,1)} fusion(bf16[480,7168]{1,0:T(8,128)(2,1)S(1)} %bitcast.46, bf16[480,256]{1,0:T(8,128)(2,1)S(1)} %get-tuple-element.14), kind=kOutput, calls=%fused_computation.5 | convolution fusion | flops 1763442688 | bytes 10797056 | tf_op jit(solution)/shard_map/dot_general | solution.py:19
  236.4 35.6 %reduce-scatter.5.cloned.1.call-done = bf16[1,60,7168]{2,1,0:T(8,128)(2,1)} async-done(((bf16[8,60,7168]{2,1,0:T(8,128)(2,1)}), bf16[1,60,7168]{2,1,0:T(8,128)(2,1)}) %reduce-scatter.5.cloned.1.call-update) | async-done | bytes 860176 | tf_op jit(solution)/shard_map/reduce_scatter | solution.py:88
  (6 shorter events, 0.0 us)
Async XLA Ops:
  7.2 53.8 %all-gather.3.cloned.1.call-start = ((), (), s32[]{:S(2)}) async-start(), calls=%async_computation.4 | async-start | bytes 8257536 | tf_op jit(solution)/shard_map/all_gather | solution.py:58
  11.9 224.4 %reduce-scatter.3.cloned.1.call-start = ((), (), s32[]{:S(2)}) async-start(), calls=%async_computation.2 | async-start | bytes 8257536 | tf_op jit(solution)/shard_map/reduce_scatter | solution.py:85
  67.9 6.1 %copy-start = (bf16[480,7168]{1,0:T(8,128)(2,1)S(1)}, bf16[480,7168]{1,0:T(8,128)(2,1)}, u32[]{:S(2)}) copy-start(bf16[480,7168]{1,0:T(8,128)(2,1)} %reshape.28) | copy-start | bytes 20643844
  67.9 7.0 %copy-start.1 = (bf16[1,7168,256]{2,1,0:T(8,128)(2,1)S(1)}, bf16[1,7168,256]{2,1,0:T(8,128)(2,1)}, u32[]{:S(2)}) copy-start(bf16[1,7168,256]{2,1,0:T(8,128)(2,1)} %param.10) | copy-start | bytes 11010052
  74.9 2.7 copy-start.3
  89.2 182.8 %reduce-scatter.5.cloned.1.call-start = ((), (), s32[]{:S(2)}) async-start(), calls=%async_computation.3 | async-start | bytes 8257536 | tf_op jit(solution)/shard_map/reduce_scatter | solution.py:88
  89.5 13.5 %collective-permute-start = (bf16[60,7168]{1,0:T(8,128)(2,1)S(1)}, bf16[60,7168]{1,0:T(8,128)(2,1)S(1)}, u32[]{:S(2)}, u32[]{:S(2)}) collective-permute-start(bf16[60,7168]{1,0:T(8,128)(2,1)S(1)} %get-tuple-element.15), channel_id=1, source_target_pairs={{0,1},{1,2},{2,3},{3,4},{4,5},{5,6},{6,7},{7,0},{8,9},{9,10},{10,1... | collective-permute-start | bytes 2580488 | tf_op jit(solution)/shard_map/ppermute | solution.py:67
  90.0 16.0 %collective-permute-start.1 = (bf16[60,7168]{1,0:T(8,128)(2,1)S(1)}, bf16[60,7168]{1,0:T(8,128)(2,1)S(1)}, u32[]{:S(2)}, u32[]{:S(2)}) collective-permute-start(bf16[60,7168]{1,0:T(8,128)(2,1)S(1)} %get-tuple-element.15), channel_id=1, source_target_pairs={{0,7},{1,0},{2,1},{3,2},{4,3},{5,4},{6,5},{7,6},{8,15},{9,8},{10,9... | collective-permute-start | bytes 2580488 | tf_op jit(solution)/shard_map/ppermute | solution.py:74
  102.9 22.7 %collective-permute-start.2 = (bf16[60,7168]{1,0:T(8,128)(2,1)S(1)}, bf16[60,7168]{1,0:T(8,128)(2,1)S(1)}, u32[]{:S(2)}, u32[]{:S(2)}) collective-permute-start(bf16[60,7168]{1,0:T(8,128)(2,1)S(1)} %collective-permute-done), channel_id=1, source_target_pairs={{0,1},{1,2},{2,3},{3,4},{4,5},{5,6},{6,7},{7,0},{8,9},{9,10},{10,1... | collective-permute-start | bytes 2580488 | tf_op jit(solution)/shard_map/ppermute | solution.py:67
  106.0 19.6 %copy-start.5 = (bf16[60,7168]{1,0:T(8,128)(2,1)}, bf16[60,7168]{1,0:T(8,128)(2,1)S(1)}, u32[]{:S(2)}) copy-start(bf16[60,7168]{1,0:T(8,128)(2,1)S(1)} %collective-permute-done.1) | copy-start | bytes 2580484
  106.0 23.1 %collective-permute-start.3 = (bf16[60,7168]{1,0:T(8,128)(2,1)S(1)}, bf16[60,7168]{1,0:T(8,128)(2,1)}, u32[]{:S(2)}, u32[]{:S(2)}) collective-permute-start(bf16[60,7168]{1,0:T(8,128)(2,1)S(1)} %collective-permute-done.1), channel_id=1, source_target_pairs={{0,7},{1,0},{2,1},{3,2},{4,3},{5,4},{6,5},{7,6},{8,15},{9,8},{10,9... | collective-permute-start | bytes 2580488 | tf_op jit(solution)/shard_map/ppermute | solution.py:74
  125.6 3.5 %copy-start.6 = (bf16[60,7168]{1,0:T(8,128)(2,1)}, bf16[60,7168]{1,0:T(8,128)(2,1)S(1)}, u32[]{:S(2)}) copy-start(bf16[60,7168]{1,0:T(8,128)(2,1)S(1)} %collective-permute-done.2) | copy-start | bytes 2580484
  125.6 22.7 %collective-permute-start.4 = (bf16[60,7168]{1,0:T(8,128)(2,1)S(1)}, bf16[60,7168]{1,0:T(8,128)(2,1)}, u32[]{:S(2)}, u32[]{:S(2)}) collective-permute-start(bf16[60,7168]{1,0:T(8,128)(2,1)S(1)} %collective-permute-done.2), channel_id=1, source_target_pairs={{0,1},{1,2},{2,3},{3,4},{4,5},{5,6},{6,7},{7,0},{8,9},{9,10},{10,1... | collective-permute-start | bytes 2580488 | tf_op jit(solution)/shard_map/ppermute | solution.py:67
  129.1 52.8 %collective-permute-start.5 = (bf16[60,7168]{1,0:T(8,128)(2,1)}, bf16[60,7168]{1,0:T(8,128)(2,1)}, u32[]{:S(2)}, u32[]{:S(2)}) collective-permute-start(bf16[60,7168]{1,0:T(8,128)(2,1)} %collective-permute-done.3), channel_id=1, source_target_pairs={{0,7},{1,0},{2,1},{3,2},{4,3},{5,4},{6,5},{7,6},{8,15},{9,8},{10,9... | collective-permute-start | bytes 2580488 | tf_op jit(solution)/shard_map/ppermute | solution.py:74
  148.4 38.3 %collective-permute-start.6 = (bf16[60,7168]{1,0:T(8,128)(2,1)}, bf16[60,7168]{1,0:T(8,128)(2,1)}, u32[]{:S(2)}, u32[]{:S(2)}) collective-permute-start(bf16[60,7168]{1,0:T(8,128)(2,1)} %collective-permute-done.4), channel_id=1, source_target_pairs={{0,1},{1,2},{2,3},{3,4},{4,5},{5,6},{6,7},{7,0},{8,9},{9,10},{10,1... | collective-permute-start | bytes 2580488 | tf_op jit(solution)/shard_map/ppermute | solution.py:67
  159.0 32.5 %copy-start.7 = (f32[480,256]{1,0:T(8,128)S(1)}, f32[480,256]{1,0:T(8,128)}, u32[]{:S(2)}) copy-start(f32[480,256]{1,0:T(8,128)} %get-tuple-element.10) | copy-start | bytes 1474564
  191.4 6.2 %copy-start.4 = (bf16[1,7168,256]{2,1,0:T(8,128)(2,1)S(1)}, bf16[1,7168,256]{2,1,0:T(8,128)(2,1)}, u32[]{:S(2)}) copy-start(bf16[1,7168,256]{2,1,0:T(8,128)(2,1)} %param.9) | copy-start | bytes 11010052
  197.6 7.0 %copy-start.2 = (bf16[1,7168,256]{2,1,0:T(8,128)(2,1)S(1)}, bf16[1,7168,256]{2,1,0:T(8,128)(2,1)}, u32[]{:S(2)}) copy-start(bf16[1,7168,256]{2,1,0:T(8,128)(2,1)} %param.10) | copy-start | bytes 11010052
  221.2 7.1 %slice-start = ((s8[6881280]{0:T(1024)(128)(4,1)}), s8[2686976]{0:T(1024)(128)(4,1)S(1)}, s32[]{:S(2)}) async-start(s8[6881280]{0:T(1024)(128)(4,1)} %bitcast.45), calls=%async_computation.5 | async-start | bytes 5373952
  221.2 7.1 %slice-start.1 = ((s8[6881280]{0:T(1024)(128)(4,1)}), s8[4194304]{0:T(1024)(128)(4,1)S(1)}, s32[]{:S(2)}) async-start(s8[6881280]{0:T(1024)(128)(4,1)} %bitcast.45), calls=%async_computation.6 | async-start | bytes 8388608
Sparse Core Ops, SparseCore 0:
  12.0 48.8 all-gather.2
  89.4 69.1 reduce-scatter.2
  221.4 50.5 reduce-scatter.4
